TPU v7x, 32 devices: a whole 2x2x4 slice. The times are simulated.
32 devices in a mesh: expert: 8 (over z, x), tensor: 4 (over y, core).
Axes of the slice: x: 2, y: 2, z: 4, core: 2. Of those that a mesh axis runs over, the one named last changes fastest.
Arguments:
- attn_heads: bfloat16 [1024, 4096], P('expert', 'tensor'), may hold values from -6 to 6
- out_proj: bfloat16 [4096, 4096], P('tensor', 'expert'), may hold values from -0.09375 to 0.09375
- residual: bfloat16 [1024, 4096], P('expert'), may hold values from -6 to 6
- norm_gain: bfloat16 [4096], replicated, may hold values from 0.099609375 to 1.8984375
- gate_proj: bfloat16 [16, 1536, 4096], P('expert', 'tensor'), may hold values from -0.09375 to 0.09375
- up_proj: bfloat16 [16, 1536, 4096], P('expert', 'tensor'), may hold values from -0.09375 to 0.09375
- down_proj: bfloat16 [16, 1536, 4096], P('expert', None, 'tensor'), may hold values from -0.15625 to 0.15625
- expert_ids: int32 [1024, 8], P('expert'), may hold values from 0 to 15, all different within a row; in each aligned block of 128 rows (0 to 127, 128 to 255, ...) at most 96 rows name the same one
- gate_scores: float32 [1024, 8], P('expert'), may hold values from 0.25 to 1
Outputs:
- layer_out: bfloat16 [1024, 4096], P('expert', 'tensor')
Inputs may be any that keep to these rules, and one draw needn't show every extreme that they name: `expert_ids`: each row names 8 different experts. Among the 128 rows of one device no expert is named by more than 96 rows, a bound that some block reaches.
All inputs are finite; a program needn't handle non-finite values.
Results may differ from a plain program's by a relative error of at most 0.0051.
Values may be sent and summed in bfloat16 or wider, within the bound.
No kernel may reach another device: no remote copies, remote signals or barrier semaphores. Data moves between devices by JAX's collectives and lax.ppermute only.
A program may use at most 128 MiB of HBM per device.

v0:
```python
import jax
import jax.numpy as jnp
from jax import lax
from jax.sharding import PartitionSpec as P

EPS = 1e-06


def on_device(
    attn_heads,
    out_proj,
    residual,
    norm_gain,
    gate_proj,
    up_proj,
    down_proj,
    expert_ids,
    gate_scores,
):
    tok_count = residual.shape[0]
    width = residual.shape[1]
    topk = expert_ids.shape[1]
    groups = lax.axis_size("expert")
    tensor_ways = lax.axis_size("tensor")
    exp_local = gate_proj.shape[0]
    experts_all = groups * exp_local
    slot_cap = 3 * tok_count * topk // (2 * experts_all)
    share = width // tensor_ways
    offset = lax.axis_index("tensor") * share
    partial_proj = jnp.dot(
        attn_heads,
        lax.all_gather(out_proj, "expert", axis=1, tiled=True),
        preferred_element_type=jnp.float32,
    )
    attn_part = lax.psum_scatter(partial_proj, "tensor", scatter_dimension=1, tiled=True)
    res_part = lax.dynamic_slice_in_dim(residual, offset, share, 1)
    state_part = (res_part.astype(jnp.float32) + attn_part).astype(jnp.bfloat16)
    state_f = state_part.astype(jnp.float32)
    squares = lax.psum(jnp.sum(state_f * state_f, axis=1), "tensor")
    gain_part = lax.dynamic_slice_in_dim(norm_gain, offset, share, 0)
    normed = (
        state_f * lax.rsqrt(squares / width + EPS)[:, None] * gain_part.astype(jnp.float32)
    ).astype(jnp.bfloat16)
    picks = expert_ids[:, :, None] == jnp.arange(experts_all, dtype=jnp.int32)[None, None, :]
    flag = jnp.sum(picks.astype(jnp.int32), axis=1)
    before = jnp.cumsum(flag, axis=0) - flag
    rank = jnp.sum(jnp.where(picks, before[:, None, :], 0), axis=2)
    slot = expert_ids * slot_cap + rank
    token_ids = jnp.arange(tok_count * topk, dtype=jnp.int32) // topk + 1
    owner = jnp.zeros((experts_all * slot_cap,), jnp.int32).at[slot.reshape(-1)].set(token_ids)
    rows = jnp.take(normed, jnp.maximum(owner - 1, 0), axis=0)
    rows = jnp.where((owner > 0)[:, None], rows, jnp.zeros((), jnp.bfloat16))
    send = rows.reshape(groups, exp_local, slot_cap, rows.shape[1])
    block = lax.all_gather(
        lax.all_to_all(send, "expert", split_axis=0, concat_axis=0, tiled=True),
        "tensor",
        axis=3,
        tiled=True,
    )
    count = block.shape[2]
    stacked = jnp.transpose(block, (1, 0, 2, 3)).reshape(exp_local, groups * count, width)
    gate = jnp.einsum("erd,efd->erf", stacked, gate_proj, preferred_element_type=jnp.float32)
    upper = jnp.einsum("erd,efd->erf", stacked, up_proj, preferred_element_type=jnp.float32)
    act = (jax.nn.silu(gate) * upper).astype(jnp.bfloat16)
    whole_act = lax.all_gather(act, "tensor", axis=2, tiled=True)
    result = jnp.einsum(
        "erf,efd->erd", whole_act, down_proj, preferred_element_type=jnp.float32
    ).astype(jnp.bfloat16)
    result = jnp.transpose(result.reshape(exp_local, groups, count, share), (1, 0, 2, 3))
    back = lax.all_to_all(result, "expert", split_axis=0, concat_axis=0, tiled=True)
    flat = back.reshape(experts_all * slot_cap, share)
    picked = jnp.take(flat, slot.reshape(-1), axis=0).reshape(tok_count, topk, share)
    weights = gate_scores / jnp.sum(gate_scores, axis=1, keepdims=True)
    mixture = jnp.einsum("tk,tkd->td", weights, picked.astype(jnp.float32))
    return (state_part.astype(jnp.float32) + mixture).astype(jnp.bfloat16)


def solution(mesh):
    in_specs = (
        P("expert", "tensor"),
        P("tensor", "expert"),
        P("expert", None),
        P(),
        P("expert", "tensor", None),
        P("expert", "tensor", None),
        P("expert", None, "tensor"),
        P("expert", None),
        P("expert", None),
    )
    out_specs = P("expert", "tensor")
    return jax.shard_map(
        on_device, mesh=mesh, in_specs=in_specs, out_specs=out_specs, check_vma=False
    )
```

profile of v0, /device:TPU:0, one launch (start us, length us, event | category | flops | bytes accessed | tf_op | source)
XLA Modules:
  0.0 507.4 jit_solution(3773535396827234200)
XLA Ops:
  6.5 0.0 copy-start
  6.5 0.0 all-gather.4.cloned.1.call-start
  6.5 0.7 all-gather.4.cloned.1.call-update
  7.3 0.0 copy-start.4
  7.3 0.0 reduce-scatter.2.cloned.1.call-start
  7.3 130.2 %all-gather.4.cloned.1.call-done = bf16[1024,4096]{1,0:T(8,128)(2,1)} async-done(((bf16[1024,512]{1,0:T(8,128)(2,1)}), bf16[1024,4096]{1,0:T(8,128)(2,1)}) %all-gather.4.cloned.1.call-update) | async-done | bytes 8388624 | tf_op jit(solution)/shard_map/all_gather | solution.py:32
  137.5 0.0 copy-done
  137.5 6.0 %fusion.14 = f32[128,4096]{1,0:T(8,128)} fusion(bf16[128,1024]{1,0:T(8,128)(2,1)S(1)} %copy-done, bf16[1024,4096]{1,0:T(8,128)(2,1)} %all-gather.4.cloned.1.call-done), kind=kOutput, calls=%fused_computation.45 | convolution fusion | flops 1073741824 | bytes 10747904 | tf_op jit(solution)/shard_map/dot_general | solution.py:30
  143.5 0.0 reduce-scatter.2.cloned.1.call-update
  143.5 0.0 all-gather.6.cloned.1.call-start
  143.6 0.0 copy-done.4
  143.6 0.1 copy.26
  143.7 0.2 reduce_window_sum.11
  143.9 0.1 copy.28
  144.0 0.1 copy.30
  144.1 0.1 reshape.84
  144.3 4.3 scatter_custom_fusion
  148.6 0.1 broadcast_in_dim.61
  148.7 0.1 broadcast_in_dim.63
  148.8 0.7 dynamic-slice_convert_fusion
  149.5 23.8 %reduce-scatter.2.cloned.1.call-done = f32[128,1024]{1,0:T(8,128)} async-done(((f32[128,4096]{1,0:T(8,128)}), f32[128,1024]{1,0:T(8,128)}) %reduce-scatter.2.cloned.1.call-update) | async-done | bytes 524304 | tf_op jit(solution)/shard_map/reduce_scatter | solution.py:35
  173.3 1.3 fusion.3
  174.6 0.0 copy-start.2
  174.6 5.8 %psum.7 = f32[128]{0:T(128)S(1)} all-reduce(f32[128]{0:T(128)S(1)} %get-tuple-element.7), channel_id=1, replica_groups=mesh['expert'=8,'tensor'=4] {'tensor'}, use_global_device_ids=true, to_apply=%region_7.8 | all-reduce | flops 128 | bytes 1024 | tf_op jit(solution)/shard_map/psum | solution.py:39
  180.3 0.0 copy-done.2
  180.4 0.1 fusion.5
  180.5 5.1 gather_fusion
  185.6 0.6 select_select_fusion
  186.2 76.2 %all_to_all.10 = bf16[8,2,96,1024]{3,2,1,0:T(8,128)(2,1)} all-to-all(bf16[8,2,96,1024]{3,2,1,0:T(8,128)(2,1)S(1)} %select_select_fusion), channel_id=1, replica_groups=mesh['expert'=8,'tensor'=4] {'expert'}, dimensions={0} | all-to-all | bytes 6291456 | tf_op jit(solution)/shard_map/all_to_all | solution.py:55
  262.4 0.0 slice-start
  262.4 0.0 all-gather.6.cloned.1.call-update
  262.5 0.2 all-gather.8.cloned.1.call-start
  262.7 80.0 %all-gather.6.cloned.1.call-done = bf16[8,2,96,4096]{3,2,1,0:T(8,128)(2,1)} async-done(((bf16[8,2,96,1024]{3,2,1,0:T(8,128)(2,1)}), bf16[8,2,96,4096]{3,2,1,0:T(8,128)(2,1)}) %all-gather.6.cloned.1.call-update) | async-done | bytes 12582928 | tf_op jit(solution)/shard_map/all_gather | solution.py:54
  342.7 0.0 slice-start.1
  342.7 6.6 %copy.31 = bf16[2,8,96,4096]{3,2,1,0:T(8,128)(2,1)S(1)} copy(bf16[2,8,96,4096]{3,2,0,1:T(8,128)(2,1)} %bitcast.26) | data formatting | bytes 25165824 | tf_op jit(solution)/shard_map/transpose | solution.py:61
  349.3 0.0 slice-done
  349.3 0.0 slice-done.1
  349.3 8.1 %fusion.15 = f32[2,768,384]{2,1,0:T(8,128)} fusion(bf16[2,768,4096]{2,1,0:T(8,128)(2,1)S(1)} %bitcast.27, bf16[2,384,4096]{2,1,0:T(8,128)(2,1)S(1)} %bitcast.35), kind=kOutput, calls=%fused_computation.46 | convolution fusion | flops 4831838208 | bytes 21233664 | tf_op jit(solution)/shard_map/erd,efd->erf/dot_general | solution.py:62
  357.4 10.0 %multiply_convert_fusion = bf16[2,768,384]{2,1,0:T(8,128)(2,1)} fusion(f32[2,768,384]{2,1,0:T(8,128)} %fusion.15, bf16[2,768,4096]{2,1,0:T(8,128)(2,1)S(1)} %bitcast.28, bf16[2,384,4096]{2,1,0:T(8,128)(2,1)} %param.14), kind=kOutput, calls=%fused_computation.5 | convolution fusion | flops 4835377152 | bytes 22413312 | tf_op jit(solution)/shard_map/erd,efd->erf/dot_general | solution.py:63
  367.4 0.0 all-gather.8.cloned.1.call-update
  367.5 37.6 %all-gather.8.cloned.1.call-done = bf16[2,768,1536]{2,1,0:T(8,128)(2,1)} async-done(((bf16[2,768,384]{2,1,0:T(8,128)(2,1)}), bf16[2,768,1536]{2,1,0:T(8,128)(2,1)}) %all-gather.8.cloned.1.call-update) | async-done | bytes 4718608 | tf_op jit(solution)/shard_map/all_gather | solution.py:65
  405.0 8.6 %convolution_convert_fusion = bf16[2,768,1024]{2,1,0:T(8,128)(2,1)S(1)} fusion(bf16[2,768,1536]{2,1,0:T(8,128)(2,1)} %all-gather.8.cloned.1.call-done, bf16[2,1536,1024]{2,1,0:T(8,128)(2,1)} %param.15), kind=kOutput, calls=%fused_computation.6 | convolution fusion | flops 4833411072 | bytes 14155776 | tf_op jit(solution)/shard_map/erf,efd->erd/dot_general | solution.py:66
  413.6 1.9 copy.37
  415.5 0.0 copy-start.5
  415.5 5.6 %all-to-all-start.1 = ((bf16[8,2,96,1024]{3,2,1,0:T(8,128)(2,1)}), bf16[8,2,96,1024]{3,2,1,0:T(8,128)(2,1)S(1)}, u32[]{:S(2)}, u32[]{:S(2)}) async-start(bf16[8,2,96,1024]{3,2,1,0:T(8,128)(2,1)} %bitcast.29), calls=%async_computation.2 | async-start | bytes 6291456 | tf_op jit(solution)/shard_map/all_to_all | solution.py:70
  421.2 0.1 copy.29
  421.3 0.0 copy-done.5
  421.3 0.1 copy.33
  421.5 70.8 %all-to-all-done.1 = bf16[8,2,96,1024]{3,2,1,0:T(8,128)(2,1)S(1)} async-done(((bf16[8,2,96,1024]{3,2,1,0:T(8,128)(2,1)}), bf16[8,2,96,1024]{3,2,1,0:T(8,128)(2,1)S(1)}, u32[]{:S(2)}, u32[]{:S(2)}) %all-to-all-start.1) | async-done | bytes 3145760 | tf_op jit(solution)/shard_map/all_to_all | solution.py:70
  492.3 0.0 copy-start.1
  492.3 5.3 %gather_fusion.1 = bf16[1024,1024]{1,0:T(8,128)(2,1)} fusion(bf16[1536,1024]{1,0:T(8,128)(2,1)S(1)} %bitcast.25, s32[1024]{0:T(1024)S(1)} %broadcast_clamp_fusion), kind=kCustom, calls=%fused_computation.1 | custom fusion | bytes 4198400 | tf_op jit(solution)/shard_map/jit(_take)/gather | solution.py:72
  497.6 0.0 copy-start.3
  497.6 2.4 fusion
  500.1 0.0 copy-done.3
  500.1 0.8 fusion.6
  500.9 0.0 copy-done.1
  (14 shorter events, 0.1 us)
Async XLA Ops:
  6.5 131.0 %copy-start = (bf16[128,1024]{1,0:T(8,128)(2,1)S(1)}, bf16[128,1024]{1,0:T(8,128)(2,1)}, u32[]{:S(2)}) copy-start(bf16[128,1024]{1,0:T(8,128)(2,1)} %param.9) | copy-start | bytes 786436
  6.5 131.0 %all-gather.4.cloned.1.call-start = ((), (), s32[]{:S(2)}) async-start(), calls=%async_computation.3 | async-start | bytes 9437184 | tf_op jit(solution)/shard_map/all_gather | solution.py:32
  7.3 136.3 %copy-start.4 = (s32[128,8]{0,1:T(8,128)S(1)}, s32[128,8]{0,1:T(8,128)}, u32[]{:S(2)}) copy-start(s32[128,8]{0,1:T(8,128)} %param.16) | copy-start | bytes 12292
  7.3 166.0 %reduce-scatter.2.cloned.1.call-start = ((), (), s32[]{:S(2)}) async-start(), calls=%async_computation.4 | async-start | bytes 2621440 | tf_op jit(solution)/shard_map/reduce_scatter | solution.py:35
  143.5 199.1 %all-gather.6.cloned.1.call-start = ((), (), s32[]{:S(2)}) async-start(), calls=%async_computation.5 | async-start | bytes 15728640 | tf_op jit(solution)/shard_map/all_gather | solution.py:54
  174.6 5.8 %copy-start.2 = (bf16[128,1024]{1,0:T(8,128)(2,1)}, bf16[128,1024]{1,0:T(8,128)(2,1)S(1)}, u32[]{:S(2)}) copy-start(bf16[128,1024]{1,0:T(8,128)(2,1)S(1)} %get-tuple-element.8) | copy-start | bytes 786436
  262.4 86.8 %slice-start = ((s8[6291456]{0:T(1024)(128)(4,1)}), s8[2097152]{0:T(1024)(128)(4,1)S(1)}, s32[]{:S(2)}) async-start(s8[6291456]{0:T(1024)(128)(4,1)} %bitcast.34), calls=%async_computation.7 | async-start | bytes 4194304
  262.5 142.5 %all-gather.8.cloned.1.call-start = ((), (), s32[]{:S(2)}) async-start(), calls=%async_computation.6 | async-start | bytes 5898240 | tf_op jit(solution)/shard_map/all_gather | solution.py:65
  342.7 6.6 %slice-start.1 = ((s8[6291456]{0:T(1024)(128)(4,1)}), s8[4194304]{0:T(1024)(128)(4,1)S(1)}, s32[]{:S(2)}) async-start(s8[6291456]{0:T(1024)(128)(4,1)} %bitcast.34), calls=%async_computation.8 | async-start | bytes 8388608
  415.5 5.8 %copy-start.5 = (f32[128,8]{0,1:T(8,128)S(1)}, f32[128,8]{0,1:T(8,128)}, u32[]{:S(2)}) copy-start(f32[128,8]{0,1:T(8,128)} %param.17) | copy-start | bytes 12292
  415.5 76.8 %all-to-all-start.1 = ((bf16[8,2,96,1024]{3,2,1,0:T(8,128)(2,1)}), bf16[8,2,96,1024]{3,2,1,0:T(8,128)(2,1)S(1)}, u32[]{:S(2)}, u32[]{:S(2)}) async-start(bf16[8,2,96,1024]{3,2,1,0:T(8,128)(2,1)} %bitcast.29), calls=%async_computation.2 | async-start | bytes 6291456 | tf_op jit(solution)/shard_map/all_to_all | solution.py:70
  492.3 8.6 %copy-start.1 = (bf16[128,1024]{1,0:T(8,128)(2,1)S(1)}, bf16[128,1024]{1,0:T(8,128)(2,1)}, u32[]{:S(2)}) copy-start(bf16[128,1024]{1,0:T(8,128)(2,1)} %param.9) | copy-start | bytes 786436
  497.6 2.4 copy-start.3
Sparse Core Ops, SparseCore 0:
  9.4 128.0 all-gather.3
  143.7 29.5 reduce-scatter.1
  262.6 80.0 all-gather.5
  367.6 37.3 all-gather.7
where the time goes:
time: 508 us; the launch traced here: 507 us
  waiting for transfers between devices  343 us (68%)
  blocking collectives  82 us (16%)
  matrix products  35.1 us (7%)
  local copies, waits for them, and re-layouts  24.1 us (5%)
  between operations  13.3 us (3%)
  starting transfers between devices  5.95 us (1%)
    all_gather x1, waiting for transfers between devices, on_device(): lax.all_gather(out_proj, 'expert', axis=1, tiled=True)  130 us
    all_gather x1, waiting for transfers between devices, on_device(): lax.all_gather(lax.all_to_all(send, 'expert', split_axis=0, concat_axis=0...  80 us
    all_to_all x1, blocking collectives, on_device(): lax.all_to_all(send, 'expert', split_axis=0, concat_axis=0, tiled=True)  76.2 us
    all_to_all x1, waiting for transfers between devices, on_device(): lax.all_to_all(result, 'expert', split_axis=0, concat_axis=0, tiled=True)  70.8 us
    all_gather x1, waiting for transfers between devices, on_device(): whole_act = lax.all_gather(act, 'tensor', axis=2, tiled=True)  37.6 us
    reduce_scatter x1, waiting for transfers between devices, on_device(): lax.psum_scatter(partial_proj, 'tensor', scatter_dimension=1, tiled=True)  23.8 us
  transfers between devices with their start and end apart: 5, of which 5 were waited for; matrix products, arithmetic and copies ran while one was open for 1% of the time, Pallas kernels for 0%

commit v1 on v0

--- a/solution.py
+++ b/solution.py
@@ -4,6 +4,22 @@
 from jax.sharding import PartitionSpec as P
 
 EPS = 1e-06
+
+
+def summed_both_ways(x, axis, dim, term):
+    size, position, rows = (lax.axis_size(axis), lax.axis_index(axis), x.shape[dim])
+    forward = [(i, (i + 1) % size) for i in range(size)]
+    downward = [(i, (i - 1) % size) for i in range(size)]
+    halfway = size // 2
+    from_left = from_right = x
+    subtotal = term(x, position * rows)
+    for hop in range(1, halfway + 1):
+        from_left = lax.ppermute(from_left, axis, forward)
+        if hop < size - halfway:
+            from_right = lax.ppermute(from_right, axis, downward)
+            subtotal = subtotal + term(from_right, (position + hop) % size * rows)
+        subtotal = subtotal + term(from_left, (position - hop) % size * rows)
+    return subtotal
 
 
 def on_device(
@@ -62,9 +78,16 @@
     gate = jnp.einsum("erd,efd->erf", stacked, gate_proj, preferred_element_type=jnp.float32)
     upper = jnp.einsum("erd,efd->erf", stacked, up_proj, preferred_element_type=jnp.float32)
     act = (jax.nn.silu(gate) * upper).astype(jnp.bfloat16)
-    whole_act = lax.all_gather(act, "tensor", axis=2, tiled=True)
-    result = jnp.einsum(
-        "erf,efd->erd", whole_act, down_proj, preferred_element_type=jnp.float32
+    result = summed_both_ways(
+        act,
+        "tensor",
+        2,
+        lambda own_block, start: jnp.einsum(
+            "erf,efd->erd",
+            own_block,
+            lax.dynamic_slice_in_dim(down_proj, start, own_block.shape[2], axis=1),
+            preferred_element_type=jnp.float32,
+        ),
     ).astype(jnp.bfloat16)
     result = jnp.transpose(result.reshape(exp_local, groups, count, share), (1, 0, 2, 3))
     back = lax.all_to_all(result, "expert", split_axis=0, concat_axis=0, tiled=True)

time: 508 us -> 505 us (level)
  waiting for transfers between devices: 343 us -> 334 us
    all_gather x1 -> x0, waiting for transfers between devices: 37.6 us -> none  [on_device(): whole_act = lax.all_gather(act, 'tensor', axis=2, tiled=True)]
    ppermute x0 -> x3, waiting for transfers between devices: none -> 31.7 us  [the longest x2 31.7 us: summed_both_ways(): from_left = lax.ppermute(from_left, axis, forward)]
    dot_general x1 -> x4, matrix products: 8.55 us -> 13.8 us  [on_device(): jnp.einsum('erf,efd->erd', own_block, lax.dynamic_slice_in_dim(down_proj,...]
  transfers between devices with their start and end apart: 5 -> 7, of which waited for: 5 -> 6; matrix products, arithmetic and copies ran while one was open for 1% -> 3% of each run, Pallas kernels for 0% -> 0%
where the time goes in v1:
time: 505 us; the launch traced here: 504 us
  waiting for transfers between devices  334 us (66%)
  blocking collectives  82 us (16%)
  matrix products  39.4 us (8%)
  local copies, waits for them, and re-layouts  24.1 us (5%)
  between operations  13.3 us (3%)
  starting transfers between devices  7.29 us (1%)
    all_gather x1, waiting for transfers between devices, on_device(): lax.all_gather(out_proj, 'expert', axis=1, tiled=True)  130 us
    all_gather x1, waiting for transfers between devices, on_device(): lax.all_gather(lax.all_to_all(send, 'expert', split_axis=0, concat_axis=0...  80.2 us
    all_to_all x1, blocking collectives, on_device(): lax.all_to_all(send, 'expert', split_axis=0, concat_axis=0, tiled=True)  76.2 us
    all_to_all x1, waiting for transfers between devices, on_device(): lax.all_to_all(result, 'expert', split_axis=0, concat_axis=0, tiled=True)  67.6 us
    ppermute x2, waiting for transfers between devices, summed_both_ways(): from_left = lax.ppermute(from_left, axis, forward)  31.7 us
    reduce_scatter x1, waiting for transfers between devices, on_device(): lax.psum_scatter(partial_proj, 'tensor', scatter_dimension=1, tiled=True)  23.8 us
    dot_general x4, matrix products, on_device(): jnp.einsum('erf,efd->erd', own_block, lax.dynamic_slice_in_dim(down_proj,...  13.8 us
  transfers between devices with their start and end apart: 7, of which 6 were waited for; matrix products, arithmetic and copies ran while one was open for 3% of the time, Pallas kernels for 0%

profile of v1, /device:TPU:0, one launch (start us, length us, event | category | flops | bytes accessed | tf_op | source)
XLA Modules:
  0.0 504.3 jit_solution(9716785739695626151)
XLA Ops:
  6.5 0.0 copy-start
  6.5 0.0 all-gather.3.cloned.1.call-start
  6.5 0.7 all-gather.3.cloned.1.call-update
  7.3 0.0 copy-start.4
  7.3 0.0 reduce-scatter.2.cloned.1.call-start
  7.3 130.2 %all-gather.3.cloned.1.call-done = bf16[1024,4096]{1,0:T(8,128)(2,1)} async-done(((bf16[1024,512]{1,0:T(8,128)(2,1)}), bf16[1024,4096]{1,0:T(8,128)(2,1)}) %all-gather.3.cloned.1.call-update) | async-done | bytes 8388624 | tf_op jit(solution)/shard_map/all_gather | solution.py:48
  137.5 0.0 copy-done
  137.5 6.0 %fusion.25 = f32[128,4096]{1,0:T(8,128)} fusion(bf16[128,1024]{1,0:T(8,128)(2,1)S(1)} %copy-done, bf16[1024,4096]{1,0:T(8,128)(2,1)} %all-gather.3.cloned.1.call-done), kind=kOutput, calls=%fused_computation.56 | convolution fusion | flops 1073741824 | bytes 10747904 | tf_op jit(solution)/shard_map/dot_general | solution.py:46
  143.5 0.0 reduce-scatter.2.cloned.1.call-update
  143.5 0.0 all-gather.5.cloned.1.call-start
  143.6 0.0 copy-done.4
  143.6 0.1 copy.26
  143.7 0.2 reduce_window_sum.11
  143.9 0.1 copy.28
  144.0 0.1 copy.30
  144.1 0.1 reshape.84
  144.3 4.3 scatter_custom_fusion
  148.6 0.1 broadcast_in_dim.61
  148.7 0.1 broadcast_in_dim.63
  148.8 0.7 dynamic-slice_convert_fusion
  149.5 23.8 %reduce-scatter.2.cloned.1.call-done = f32[128,1024]{1,0:T(8,128)} async-done(((f32[128,4096]{1,0:T(8,128)}), f32[128,1024]{1,0:T(8,128)}) %reduce-scatter.2.cloned.1.call-update) | async-done | bytes 524304 | tf_op jit(solution)/shard_map/reduce_scatter | solution.py:51
  173.3 1.3 fusion.10
  174.6 0.0 copy-start.2
  174.6 5.8 %psum.7 = f32[128]{0:T(128)S(1)} all-reduce(f32[128]{0:T(128)S(1)} %get-tuple-element.7), channel_id=1, replica_groups=mesh['expert'=8,'tensor'=4] {'tensor'}, use_global_device_ids=true, to_apply=%region_7.8 | all-reduce | flops 128 | bytes 1024 | tf_op jit(solution)/shard_map/psum | solution.py:55
  180.3 0.0 copy-done.2
  180.4 0.1 fusion.12
  180.5 5.1 %gather_fusion = bf16[1536,1024]{1,0:T(8,128)(2,1)S(1)} fusion(bf16[128,1024]{1,0:T(8,128)(2,1)S(1)} %fusion.12, s32[2048]{0:T(1024)S(1)} %pad_clamp_fusion), kind=kCustom, calls=%fused_computation | custom fusion | bytes 6297600 | tf_op jit(solution)/shard_map/jit(_take)/gather | solution.py:67
  185.6 0.6 select_select_fusion
  186.2 76.2 %all_to_all.10 = bf16[8,2,96,1024]{3,2,1,0:T(8,128)(2,1)} all-to-all(bf16[8,2,96,1024]{3,2,1,0:T(8,128)(2,1)S(1)} %select_select_fusion), channel_id=1, replica_groups=mesh['expert'=8,'tensor'=4] {'expert'}, dimensions={0} | all-to-all | bytes 6291456 | tf_op jit(solution)/shard_map/all_to_all | solution.py:71
  262.4 0.0 slice-start
  262.4 0.0 all-gather.5.cloned.1.call-update
  262.5 80.2 %all-gather.5.cloned.1.call-done = bf16[8,2,96,4096]{3,2,1,0:T(8,128)(2,1)} async-done(((bf16[8,2,96,1024]{3,2,1,0:T(8,128)(2,1)}), bf16[8,2,96,4096]{3,2,1,0:T(8,128)(2,1)}) %all-gather.5.cloned.1.call-update) | async-done | bytes 12582928 | tf_op jit(solution)/shard_map/all_gather | solution.py:70
  342.7 0.0 slice-start.1
  342.7 6.6 %copy.31 = bf16[2,8,96,4096]{3,2,1,0:T(8,128)(2,1)S(1)} copy(bf16[2,8,96,4096]{3,2,0,1:T(8,128)(2,1)} %bitcast.28) | data formatting | bytes 25165824 | tf_op jit(solution)/shard_map/transpose | solution.py:77
  349.3 0.0 slice-done
  349.3 0.0 slice-done.1
  349.3 8.1 %fusion.26 = f32[2,768,384]{2,1,0:T(8,128)} fusion(bf16[2,768,4096]{2,1,0:T(8,128)(2,1)S(1)} %bitcast.29, bf16[2,384,4096]{2,1,0:T(8,128)(2,1)S(1)} %bitcast.37), kind=kOutput, calls=%fused_computation.57 | convolution fusion | flops 4831838208 | bytes 21233664 | tf_op jit(solution)/shard_map/erd,efd->erf/dot_general | solution.py:78
  357.4 9.2 %multiply_convert_fusion = bf16[2,768,384]{2,1,0:T(8,128)(2,1)S(1)} fusion(f32[2,768,384]{2,1,0:T(8,128)} %fusion.26, bf16[2,768,4096]{2,1,0:T(8,128)(2,1)S(1)} %bitcast.30, bf16[2,384,4096]{2,1,0:T(8,128)(2,1)} %param.14), kind=kOutput, calls=%fused_computation.6 | convolution fusion | flops 4835377152 | bytes 22413312 | tf_op jit(solution)/shard_map/erd,efd->erf/dot_general | solution.py:79
  366.6 0.3 collective-permute-start.1
  366.9 1.5 collective-permute-start
  368.4 26.0 %collective-permute-done.1 = bf16[2,768,384]{2,1,0:T(8,128)(2,1)S(1)} collective-permute-done((bf16[2,768,384]{2,1,0:T(8,128)(2,1)S(1)}, bf16[2,768,384]{2,1,0:T(8,128)(2,1)S(1)}, u32[]{:S(2)}, u32[]{:S(2)}) %collective-permute-start.1) | collective-permute-done | bytes 1179680 | tf_op jit(solution)/shard_map/ppermute | solution.py:17
  394.3 0.0 collective-permute-start.2
  394.3 3.2 fusion.7
  397.5 3.2 fusion.3
  400.8 0.0 collective-permute-done
  400.8 3.6 fusion.5
  404.3 5.7 %collective-permute-done.2 = bf16[2,768,384]{2,1,0:T(8,128)(2,1)} collective-permute-done((bf16[2,768,384]{2,1,0:T(8,128)(2,1)S(1)}, bf16[2,768,384]{2,1,0:T(8,128)(2,1)}, u32[]{:S(2)}, u32[]{:S(2)}) %collective-permute-start.2) | collective-permute-done | bytes 1179680 | tf_op jit(solution)/shard_map/ppermute | solution.py:17
  410.1 3.8 add_convert_fusion
  413.9 2.0 copy.37
  415.9 0.0 copy-start.5
  415.9 5.4 %all-to-all-start.1 = ((bf16[8,2,96,1024]{3,2,1,0:T(8,128)(2,1)}), bf16[8,2,96,1024]{3,2,1,0:T(8,128)(2,1)S(1)}, u32[]{:S(2)}, u32[]{:S(2)}) async-start(bf16[8,2,96,1024]{3,2,1,0:T(8,128)(2,1)} %bitcast.31), calls=%async_computation.2 | async-start | bytes 6291456 | tf_op jit(solution)/shard_map/all_to_all | solution.py:93
  421.3 0.1 copy.29
  421.4 0.0 copy-done.5
  421.4 0.1 copy.33
  421.6 67.6 %all-to-all-done.1 = bf16[8,2,96,1024]{3,2,1,0:T(8,128)(2,1)S(1)} async-done(((bf16[8,2,96,1024]{3,2,1,0:T(8,128)(2,1)}), bf16[8,2,96,1024]{3,2,1,0:T(8,128)(2,1)S(1)}, u32[]{:S(2)}, u32[]{:S(2)}) %all-to-all-start.1) | async-done | bytes 3145760 | tf_op jit(solution)/shard_map/all_to_all | solution.py:93
  489.2 0.0 copy-start.1
  489.2 5.3 %gather_fusion.1 = bf16[1024,1024]{1,0:T(8,128)(2,1)} fusion(bf16[1536,1024]{1,0:T(8,128)(2,1)S(1)} %bitcast.27, s32[1024]{0:T(1024)S(1)} %broadcast_clamp_fusion), kind=kCustom, calls=%fused_computation.1 | custom fusion | bytes 4198400 | tf_op jit(solution)/shard_map/jit(_take)/gather | solution.py:95
  494.5 0.0 copy-start.3
  494.5 2.4 fusion
  497.0 0.0 copy-done.3
  497.0 0.8 fusion.13
  497.8 0.0 copy-done.1
  (14 shorter events, 0.1 us)
Async XLA Ops:
  6.5 131.0 %copy-start = (bf16[128,1024]{1,0:T(8,128)(2,1)S(1)}, bf16[128,1024]{1,0:T(8,128)(2,1)}, u32[]{:S(2)}) copy-start(bf16[128,1024]{1,0:T(8,128)(2,1)} %param.9) | copy-start | bytes 786436
  6.5 131.0 %all-gather.3.cloned.1.call-start = ((), (), s32[]{:S(2)}) async-start(), calls=%async_computation.3 | async-start | bytes 9437184 | tf_op jit(solution)/shard_map/all_gather | solution.py:48
  7.3 136.3 %copy-start.4 = (s32[128,8]{0,1:T(8,128)S(1)}, s32[128,8]{0,1:T(8,128)}, u32[]{:S(2)}) copy-start(s32[128,8]{0,1:T(8,128)} %param.16) | copy-start | bytes 12292
  7.3 166.0 %reduce-scatter.2.cloned.1.call-start = ((), (), s32[]{:S(2)}) async-start(), calls=%async_computation.4 | async-start | bytes 2621440 | tf_op jit(solution)/shard_map/reduce_scatter | solution.py:51
  143.5 199.1 %all-gather.5.cloned.1.call-start = ((), (), s32[]{:S(2)}) async-start(), calls=%async_computation.5 | async-start | bytes 15728640 | tf_op jit(solution)/shard_map/all_gather | solution.py:70
  174.6 5.8 %copy-start.2 = (bf16[128,1024]{1,0:T(8,128)(2,1)}, bf16[128,1024]{1,0:T(8,128)(2,1)S(1)}, u32[]{:S(2)}) copy-start(bf16[128,1024]{1,0:T(8,128)(2,1)S(1)} %get-tuple-element.8) | copy-start | bytes 786436
  262.4 86.8 %slice-start = ((s8[6291456]{0:T(1024)(128)(4,1)}), s8[2097152]{0:T(1024)(128)(4,1)S(1)}, s32[]{:S(2)}) async-start(s8[6291456]{0:T(1024)(128)(4,1)} %bitcast.36), calls=%async_computation.6 | async-start | bytes 4194304
  342.7 6.6 %slice-start.1 = ((s8[6291456]{0:T(1024)(128)(4,1)}), s8[4194304]{0:T(1024)(128)(4,1)S(1)}, s32[]{:S(2)}) async-start(s8[6291456]{0:T(1024)(128)(4,1)} %bitcast.36), calls=%async_computation.7 | async-start | bytes 8388608
  366.6 27.8 %collective-permute-start.1 = (bf16[2,768,384]{2,1,0:T(8,128)(2,1)S(1)}, bf16[2,768,384]{2,1,0:T(8,128)(2,1)S(1)}, u32[]{:S(2)}, u32[]{:S(2)}) collective-permute-start(bf16[2,768,384]{2,1,0:T(8,128)(2,1)S(1)} %multiply_convert_fusion), channel_id=1, source_target_pairs={{0,1},{1,2},{2,3},{3,0},{4,5},{5,6},{6,7},{7,4},{8,9},{9,10},{10,1... | collective-permute-start | bytes 3538952 | tf_op jit(solution)/shard_map/ppermute | solution.py:17
  366.9 33.9 %collective-permute-start = (bf16[2,768,384]{2,1,0:T(8,128)(2,1)S(1)}, bf16[2,768,384]{2,1,0:T(8,128)(2,1)}, u32[]{:S(2)}, u32[]{:S(2)}) collective-permute-start(bf16[2,768,384]{2,1,0:T(8,128)(2,1)S(1)} %multiply_convert_fusion), channel_id=1, source_target_pairs={{0,3},{1,0},{2,1},{3,2},{4,7},{5,4},{6,5},{7,6},{8,11},{9,8},{10,9... | collective-permute-start | bytes 3538952 | tf_op jit(solution)/shard_map/ppermute | solution.py:19
  394.3 15.7 %collective-permute-start.2 = (bf16[2,768,384]{2,1,0:T(8,128)(2,1)S(1)}, bf16[2,768,384]{2,1,0:T(8,128)(2,1)}, u32[]{:S(2)}, u32[]{:S(2)}) collective-permute-start(bf16[2,768,384]{2,1,0:T(8,128)(2,1)S(1)} %collective-permute-done.1), channel_id=1, source_target_pairs={{0,1},{1,2},{2,3},{3,0},{4,5},{5,6},{6,7},{7,4},{8,9},{9,10},{10,1... | collective-permute-start | bytes 3538952 | tf_op jit(solution)/shard_map/ppermute | solution.py:17
  415.9 5.5 %copy-start.5 = (f32[128,8]{0,1:T(8,128)S(1)}, f32[128,8]{0,1:T(8,128)}, u32[]{:S(2)}) copy-start(f32[128,8]{0,1:T(8,128)} %param.17) | copy-start | bytes 12292
  415.9 73.3 %all-to-all-start.1 = ((bf16[8,2,96,1024]{3,2,1,0:T(8,128)(2,1)}), bf16[8,2,96,1024]{3,2,1,0:T(8,128)(2,1)S(1)}, u32[]{:S(2)}, u32[]{:S(2)}) async-start(bf16[8,2,96,1024]{3,2,1,0:T(8,128)(2,1)} %bitcast.31), calls=%async_computation.2 | async-start | bytes 6291456 | tf_op jit(solution)/shard_map/all_to_all | solution.py:93
  489.2 8.6 %copy-start.1 = (bf16[128,1024]{1,0:T(8,128)(2,1)S(1)}, bf16[128,1024]{1,0:T(8,128)(2,1)}, u32[]{:S(2)}) copy-start(bf16[128,1024]{1,0:T(8,128)(2,1)} %param.9) | copy-start | bytes 786436
  494.5 2.4 copy-start.3
Sparse Core Ops, SparseCore 0:
  9.4 128.0 all-gather.2
  143.7 29.5 reduce-scatter.1
  262.6 80.0 all-gather.4
